TPU v7x, 256 devices: a whole 4x4x8 slice. The times are simulated.
256 devices in a mesh: kv: 8 (over z), blk: 32 (over y, x, core).
Axes of the slice: x: 4, y: 4, z: 8, core: 2. Of those that a mesh axis runs over, the one named last changes fastest.
Arguments:
- hidden_in: bfloat16 [4, 16, 4096], P(None, None, 'blk'), may hold values from -6 to 6
- attn_gain: bfloat16 [4096], P('blk'), may hold values from 0.5 to 1.5
- ffn_gain: bfloat16 [4096], replicated, may hold values from 0.5 to 1.5
- query_key_value_weight: bfloat16 [4096, 8, 768], P('blk', 'kv'), may hold values from -0.09375 to 0.09375
- out_weight: bfloat16 [4096, 4096], P('kv', 'blk'), may hold values from -0.09375 to 0.09375
- router_weight: bfloat16 [4096, 8], replicated, may hold values from -0.09375 to 0.09375
- expert_in: bfloat16 [8, 4096, 2, 8192], P('kv', None, None, 'blk'), may hold values from -0.09375 to 0.09375
- expert_down: bfloat16 [8, 8192, 4096], P('kv', 'blk'), may hold values from -0.125 to 0.125
- kv_cache: bfloat16 [2048, 2, 8, 128, 128], P('blk', None, 'kv')
- lengths: int32 [2], replicated, may hold values from 1 to 16384, as said below
- tables: int32 [16, 128], replicated, may hold values from 0 to 2047, as said below
- parents: int32 [4, 16], replicated, may hold values from 0 to 15, as said below
- routes: int32 [4, 16, 2], replicated, may hold values from 0 to 7, all different within a row; in each aligned block of 16 rows (0 to 15, 16 to 31, ..., all dimensions but the last counted through in order) at most 6 rows name the same one
Outputs:
- layer_out: bfloat16 [4, 16, 4096], P(None, None, 'blk')
Inputs may be any that keep to these rules, and one draw needn't show every extreme that they name: `lengths`: one group has exactly 16384 cached positions. `tables`: each pool block is named exactly once. `parents`: a beam's parent is a beam of its own group of 8 consecutive beams. `routes`: in each step no expert is named by more than 6 beams, a bound that some block reaches.
All inputs are finite; a program needn't handle non-finite values.
Results may differ from a plain program's by a relative error of at most 0.013.
Values may be sent and summed in bfloat16 or wider, within the bound.
No kernel may reach another device: no remote copies, remote signals or barrier semaphores. Data moves between devices by JAX's collectives and lax.ppermute only.
A program may use at most 64 MiB of HBM per device.

v0:
```python
import math
import jax
import jax.numpy as jnp
from jax import lax
from jax.sharding import PartitionSpec as P

MODEL_WIDTH = 4096
HEAD_WIDTH = 128
QUERIES_PER_KEY = 4
EXPERTS = 8
BEAM_W = 8
GROUPS = 2
DECODE_STEPS = 4
BLOCK_POSITIONS = 128
BEAM_BLOCKS = 128
BEAM_TOTAL = 16
CAP = 6
NORM_FLOOR = 1e-05
ROPE_BASE = 1000000.0
NEG_FILL = -1e30


def joined(value, axis, join):
    pieces = jax.tree.map(lambda part: lax.all_gather(part, axis), value)
    head = jax.tree.map(lambda part: part[0], pieces)
    tail = jax.tree.map(lambda part: part[1:], pieces)
    running, _ = lax.scan(lambda running, section: (join(running, section), None), head, tail)
    return running


def rotate_pairs(vectors, positions):
    half_width = vectors.shape[-1] // 2
    exponents = jnp.arange(half_width, dtype=jnp.float32) * (2.0 / vectors.shape[-1])
    frequency = ROPE_BASE ** (-exponents)
    angles = positions.astype(jnp.float32)[..., None] * frequency
    cosine = jnp.cos(angles)
    sine_part = jnp.sin(angles)
    lower_half = vectors[..., :half_width]
    upper_half = vectors[..., half_width:]
    return jnp.concatenate(
        [
            lower_half * cosine - upper_half * sine_part,
            upper_half * cosine + lower_half * sine_part,
        ],
        axis=-1,
    )


def lineage(parents):
    steps_count, beam_count = parents.shape
    beam_ids = jnp.arange(beam_count, dtype=jnp.int32)
    line_rows = []
    anchor_rows = []
    for step_index in range(steps_count):
        current = beam_ids
        levels = [jnp.full((beam_count,), -1, jnp.int32) for level_index in range(steps_count)]
        for level_index in range(step_index, -1, -1):
            levels[level_index] = current
            current = parents[level_index][current]
        line_rows.append(jnp.stack(levels))
        anchor_rows.append(current)
    return (jnp.stack(line_rows), jnp.stack(anchor_rows))


def expert_rank(routes):
    steps_count, beam_count, pick_count = routes.shape
    onehot = (routes[..., None] == jnp.arange(EXPERTS, dtype=jnp.int32)).astype(jnp.int32)
    flat_hits = onehot.reshape(steps_count, beam_count * pick_count, EXPERTS)
    before = jnp.cumsum(flat_hits, axis=1) - flat_hits
    return jnp.sum(before * flat_hits, axis=-1).reshape(steps_count, beam_count, pick_count)


def head_total(partial_value):
    return lax.psum(partial_value, "kv")


def combine_parts(part_one, part_two):
    max_one, sum_one, vector_one = part_one
    max_two, sum_two, vector_two = part_two
    larger = jnp.maximum(max_one, max_two)
    scale_one = jnp.exp(max_one - larger)
    scale_two = jnp.exp(max_two - larger)
    return (
        larger,
        sum_one * scale_one + sum_two * scale_two,
        vector_one * scale_one[..., None] + vector_two * scale_two[..., None],
    )


def groups_to_beams(grouped):
    shaped = grouped.reshape((GROUPS, DECODE_STEPS, BEAM_W, QUERIES_PER_KEY) + grouped.shape[2:])
    shaped = jnp.moveaxis(shaped, 1, 0)
    return shaped.reshape((DECODE_STEPS, BEAM_TOTAL, QUERIES_PER_KEY) + grouped.shape[2:])


def body(
    hidden_in,
    attn_gain,
    ffn_gain,
    query_key_value_weight,
    out_weight,
    router_weight,
    expert_in,
    expert_down,
    kv_cache,
    lengths,
    tables,
    parents,
    routes,
):
    count_tokens = DECODE_STEPS * BEAM_TOTAL
    width_local = hidden_in.shape[2]
    heads_local = query_key_value_weight.shape[1]
    logit_scale = 1.0 / math.sqrt(HEAD_WIDTH)
    line_beams, anchor = lineage(parents)
    flat_in = hidden_in.reshape(count_tokens, width_local).astype(jnp.float32)
    pre_attn = (flat_in * attn_gain.astype(jnp.float32)).astype(jnp.bfloat16)
    partial_proj = jnp.dot(
        pre_attn,
        query_key_value_weight.reshape(width_local, -1),
        preferred_element_type=jnp.float32,
    )
    partial_sq = jnp.sum(flat_in * flat_in, axis=1)
    projected_rows, square_sum = lax.psum((partial_proj, partial_sq), "blk")
    projected_rows = (
        projected_rows * lax.rsqrt(square_sum / MODEL_WIDTH + NORM_FLOOR)[:, None]
    ).reshape(DECODE_STEPS, BEAM_TOTAL, heads_local, QUERIES_PER_KEY + 2, HEAD_WIDTH)
    beam_groups = jnp.arange(BEAM_TOTAL, dtype=jnp.int32) // BEAM_W
    positions = lengths[beam_groups][None, :] + jnp.arange(DECODE_STEPS, dtype=jnp.int32)[:, None]
    queries = rotate_pairs(
        projected_rows[:, :, :, :QUERIES_PER_KEY], positions[:, :, None, None]
    ).astype(jnp.bfloat16)
    new_key = rotate_pairs(projected_rows[:, :, :, QUERIES_PER_KEY], positions[:, :, None]).astype(
        jnp.bfloat16
    )
    new_value = projected_rows[:, :, :, QUERIES_PER_KEY + 1].astype(jnp.bfloat16)
    slot_count = kv_cache.shape[0]
    slot_base = lax.axis_index("blk") * slot_count
    entry_ids = jnp.arange(BEAM_TOTAL * BEAM_BLOCKS, dtype=jnp.int32)
    owner_all = (
        jnp.zeros((BEAM_TOTAL * BEAM_BLOCKS,), jnp.int32)
        .at[tables.reshape(-1)]
        .set(entry_ids // BEAM_BLOCKS)
    )
    block_all = (
        jnp.zeros((BEAM_TOTAL * BEAM_BLOCKS,), jnp.int32)
        .at[tables.reshape(-1)]
        .set(entry_ids % BEAM_BLOCKS)
    )
    owner_here = lax.dynamic_slice_in_dim(owner_all, slot_base, slot_count)
    block_here = lax.dynamic_slice_in_dim(block_all, slot_base, slot_count)
    group_here = owner_here // BEAM_W
    live_keys = (
        block_here[:, None] * BLOCK_POSITIONS
        + jnp.arange(BLOCK_POSITIONS, dtype=jnp.int32)[None, :]
        < lengths[group_here][:, None]
    )
    anchor_groups = jnp.moveaxis(anchor.reshape(DECODE_STEPS, GROUPS, BEAM_W), 1, 0)
    anchor_query = jnp.broadcast_to(
        anchor_groups[..., None], (GROUPS, DECODE_STEPS, BEAM_W, QUERIES_PER_KEY)
    ).reshape(GROUPS, -1)
    query_match = anchor_query[group_here] == owner_here[:, None]
    group_hits = group_here[:, None] == jnp.arange(GROUPS, dtype=jnp.int32)[None, :]
    group_float = group_hits.astype(jnp.float32)
    recent_allowed = jnp.transpose(
        line_beams[:, :, :, None] == jnp.arange(BEAM_TOTAL, dtype=jnp.int32), (0, 2, 1, 3)
    ).reshape(DECODE_STEPS, BEAM_TOTAL, 1, count_tokens)
    is_first = lax.axis_index("blk") == 0
    query_head = queries[:, :, 0]
    query_groups = jnp.moveaxis(
        query_head.reshape(DECODE_STEPS, GROUPS, BEAM_W, QUERIES_PER_KEY, HEAD_WIDTH), 1, 0
    ).reshape(GROUPS, -1, HEAD_WIDTH)
    query_slots = query_groups[group_here]
    key_matrix = kv_cache[:, 0, 0]
    value_matrix = kv_cache[:, 1, 0]
    scores = (
        jnp.einsum("ptd,pqd->ptq", key_matrix, query_slots, preferred_element_type=jnp.float32)
        * logit_scale
    )
    allowed = live_keys[:, :, None] & query_match[:, None, :]
    masked = jnp.where(allowed, scores, NEG_FILL)
    slot_max = jnp.max(masked, axis=1)
    weights = jnp.where(allowed, jnp.exp(masked - slot_max[:, None, :]), 0.0)
    slot_sum = jnp.sum(weights, axis=1)
    slot_vector = jnp.einsum(
        "ptq,ptd->pqd",
        weights.astype(jnp.bfloat16),
        value_matrix,
        preferred_element_type=jnp.float32,
    )
    group_max = jnp.max(jnp.where(group_hits[:, :, None], slot_max[:, None, :], NEG_FILL), axis=0)
    rescale = jnp.exp(slot_max - group_max[group_here])
    group_sum = jnp.einsum(
        "pg,pq->gq", group_float, slot_sum * rescale, precision=lax.Precision.HIGHEST
    )
    group_vector = jnp.einsum(
        "pg,pqd->gqd",
        group_float,
        slot_vector * rescale[:, :, None],
        precision=lax.Precision.HIGHEST,
    )
    cache_max = groups_to_beams(group_max)
    cache_sum = groups_to_beams(group_sum)
    cache_vector = groups_to_beams(group_vector)
    newest_keys = new_key[:, :, 0].reshape(count_tokens, HEAD_WIDTH)
    newest_values = new_value[:, :, 0].reshape(count_tokens, HEAD_WIDTH)
    newest_logits = (
        jnp.einsum("sbqd,kd->sbqk", query_head, newest_keys, preferred_element_type=jnp.float32)
        * logit_scale
    )
    recent_masked = jnp.where(recent_allowed, newest_logits, NEG_FILL)
    recent_max = jnp.max(recent_masked, axis=-1)
    recent_weights = jnp.where(recent_allowed, jnp.exp(recent_masked - recent_max[..., None]), 0.0)
    recent_sum = jnp.sum(recent_weights, axis=-1)
    recent_vector = jnp.einsum(
        "sbqk,kd->sbqd",
        recent_weights.astype(jnp.bfloat16),
        newest_values,
        preferred_element_type=jnp.float32,
    )
    recent_max = jnp.where(is_first, recent_max, NEG_FILL)
    recent_sum = jnp.where(is_first, recent_sum, 0.0)
    recent_vector = jnp.where(is_first, recent_vector, 0.0)
    local_max, local_sum, local_vector = combine_parts(
        (cache_max, cache_sum, cache_vector), (recent_max, recent_sum, recent_vector)
    )
    max_heads = [local_max]
    sum_heads = [local_sum]
    vector_heads = [local_vector]
    part_max = jnp.stack(max_heads, axis=2)
    part_sum = jnp.stack(sum_heads, axis=2)
    part_vector = jnp.stack(vector_heads, axis=2)
    whole_max, whole_sum, whole_vector = joined(
        (part_max, part_sum, part_vector), "blk", combine_parts
    )
    attended_rows = (
        (whole_vector / whole_sum[..., None]).astype(jnp.bfloat16).reshape(count_tokens, -1)
    )
    attn_partial = jnp.dot(attended_rows, out_weight, preferred_element_type=jnp.float32)
    attn_out = head_total(attn_partial)
    residual = (flat_in + attn_out).astype(jnp.bfloat16)
    experts_local = expert_in.shape[0]
    ff_local = expert_in.shape[3]
    rows_per_expert = DECODE_STEPS * CAP
    rows_local = experts_local * rows_per_expert
    flat_routes = routes.reshape(count_tokens, 2)
    rank = expert_rank(routes).reshape(count_tokens, 2)
    step_of = jnp.arange(count_tokens, dtype=jnp.int32) // BEAM_TOTAL
    row_id = (flat_routes * rows_per_expert + step_of[:, None] * CAP + rank).reshape(-1)
    token_ids = jnp.broadcast_to(
        jnp.arange(count_tokens, dtype=jnp.int32)[:, None], (count_tokens, 2)
    ).reshape(-1)
    table_size = EXPERTS * rows_per_expert
    row_token_all = jnp.zeros((table_size,), jnp.int32).at[row_id].set(token_ids)
    row_live_all = jnp.zeros((table_size,), jnp.float32).at[row_id].set(1.0)
    row_other_all = (
        jnp.zeros((table_size,), jnp.int32).at[row_id].set(flat_routes[:, ::-1].reshape(-1))
    )
    row_start = lax.axis_index("kv") * rows_local
    row_token = lax.dynamic_slice_in_dim(row_token_all, row_start, rows_local)
    row_live = lax.dynamic_slice_in_dim(row_live_all, row_start, rows_local)
    row_other = lax.dynamic_slice_in_dim(row_other_all, row_start, rows_local)
    row_own = (row_start + jnp.arange(rows_local, dtype=jnp.int32)) // rows_per_expert
    in_flat = expert_in.reshape(experts_local, MODEL_WIDTH, 2 * ff_local)
    gain_wide = ffn_gain.astype(jnp.float32)
    full_rows = lax.all_gather(residual, "blk", axis=1, tiled=True)
    chosen = full_rows[row_token].astype(jnp.float32)
    pre_rows = (chosen * gain_wide).astype(jnp.bfloat16)
    sums_in = jnp.einsum(
        "erd,edf->erf",
        pre_rows.reshape(experts_local, rows_per_expert, MODEL_WIDTH),
        in_flat,
        preferred_element_type=jnp.float32,
    )
    sums_router = jnp.dot(pre_rows, router_weight, preferred_element_type=jnp.float32)
    sum_sq = jnp.sum(chosen * chosen, axis=1)
    inv_rows = lax.rsqrt(sum_sq / MODEL_WIDTH + NORM_FLOOR)
    expert_act = sums_in * inv_rows.reshape(experts_local, rows_per_expert)[:, :, None]
    expert_hidden = (jax.nn.silu(expert_act[..., :ff_local]) * expert_act[..., ff_local:]).astype(
        jnp.bfloat16
    )
    down_part = jnp.einsum(
        "erf,efd->erd", expert_hidden, expert_down, preferred_element_type=jnp.float32
    ).reshape(rows_local, MODEL_WIDTH)
    expert_result = lax.psum_scatter(down_part, "blk", scatter_dimension=1, tiled=True)
    logits = sums_router * inv_rows[:, None]
    expert_ids = jnp.arange(EXPERTS, dtype=jnp.int32)
    own_logit = jnp.sum(jnp.where(row_own[:, None] == expert_ids[None, :], logits, 0.0), axis=1)
    other_logit = jnp.sum(jnp.where(row_other[:, None] == expert_ids[None, :], logits, 0.0), axis=1)
    gate_share = row_live / (1.0 + jnp.exp(other_logit - own_logit))
    weighted_values = expert_result * gate_share[:, None]
    placement = (row_token[None, :] == jnp.arange(count_tokens, dtype=jnp.int32)[:, None]).astype(
        jnp.float32
    )
    mixture_part = jnp.dot(placement, weighted_values, precision=lax.Precision.HIGHEST)
    mixture = head_total(mixture_part)
    layer_out = (residual.astype(jnp.float32) + mixture).astype(jnp.bfloat16)
    return layer_out.reshape(DECODE_STEPS, BEAM_TOTAL, width_local)


def solution(mesh):
    placed = (
        P(None, None, "blk"),
        P("blk"),
        P(),
        P("blk", "kv", None),
        P("kv", "blk"),
        P(),
        P("kv", None, None, "blk"),
        P("kv", "blk", None),
        P("blk", None, "kv", None, None),
        P(),
        P(),
        P(),
        P(),
    )
    return jax.shard_map(
        body, mesh=mesh, in_specs=placed, out_specs=P(None, None, "blk"), check_vma=False
    )
```

profile of v0, /device:TPU:2, one launch (start us, length us, event | category | flops | bytes accessed | tf_op | source)
XLA Modules:
  0.0 434.0 jit_solution(2719535748926274330)
XLA Ops:
  7.3 0.8 multiply_reduce_fusion
  8.2 1.8 fusion.31
  10.0 1.3 fusion.108
  12.1 8.0 %scatter_custom_fusion = s32[2048]{0:T(1024)S(1)} fusion(s32[2048]{0:T(1024)S(1)} %bitcast.249, s32[2048]{0:T(1024)S(1)} %add_select_fusion, s32[]{:T(128)} %constant.125.clone.1), kind=kCustom, calls=%fused_computation.168 | custom fusion | bytes 8196 | tf_op jit(solution)/shard_map/scatter | solution.py:143
  20.1 8.0 %scatter_custom_fusion.1 = s32[2048]{0:T(1024)S(1)} fusion(s32[2048]{0:T(1024)S(1)} %bitcast.250, s32[2048]{0:T(1024)S(1)} %fusion.64, s32[]{:T(128)} %constant.125.clone.1), kind=kCustom, calls=%fused_computation.166 | custom fusion | bytes 8196 | tf_op jit(solution)/shard_map/scatter | solution.py:148
  28.2 1.3 fusion.86
  29.5 1.4 compare_select_fusion.12
  31.0 0.8 slice_bitcast_fusion.5
  39.1 62.3 %psum.29 = f32[64]{0:T(128)S(1)} all-reduce(f32[64]{0:T(128)S(1)} %reduce_sum.66), channel_id=1, replica_groups=mesh['kv'=8,'blk'=32] {'blk'}, use_global_device_ids=true, to_apply=%region_4.5 | all-reduce | flops 64 | bytes 512 | tf_op jit(solution)/shard_map/psum | solution.py:124
  103.0 21.4 %all-reduce.2.cloned.1.call-done = f32[64,768]{1,0:T(8,128)} async-done(((f32[64,768]{1,0:T(8,128)}), f32[64,768]{1,0:T(8,128)}) %all-reduce.2.cloned.1.call-update) | async-done | bytes 196624 | tf_op jit(solution)/shard_map/psum | solution.py:124
  124.4 1.0 broadcast_multiply_fusion
  125.9 2.2 gather_fusion.11
  128.0 4.6 %fusion.8 = (f32[64,128]{1,0:T(8,128)S(1)}, f32[64,128,128]{1,2,0:T(8,128)}) fusion(pred[64,128]{1,0:T(8,128)(4,1)S(1)} %broadcast_compare_fusion.1, pred[64,128]{1,0:T(8,128)(4,1)S(1)} %add_compare_fusion, bf16[64,128,128]{2,1,0:T(8,128)(2,1)} %gather_fusion.11, bf16[64,2,1,128,128]{4,3,2,1,0:T(8,128)(2,1)} %param.23), kind=kOutput, calls=%fused_computation.35 | convolution fusion | flops 272621568 | bytes 8437760 | tf_op jit(solution)/shard_map/ptd,pqd->ptq/dot_general | solution.py:177
  133.9 5.8 %convolution_multiply_fusion = f32[64,128,128]{2,1,0:T(8,128)S(1)} fusion(f32[64,128,128]{1,2,0:T(8,128)} %get-tuple-element.131, f32[64,128]{1,0:T(8,128)S(1)} %subtract_exponential_fusion.1, bf16[64,2,1,128,128]{4,3,2,1,0:T(8,128)(2,1)} %param.23, f32[64,128]{1,0:T(8,128)S(1)} %get-tuple-element.130, pred[64,128]{1,0:T(8,128)(4,1)S(1)} %broadcast_compare_fusion.1, ...), kind=kOutput, calls=%fused_computation.38 | convolution fusion | flops 275775488 | bytes 10567680 | tf_op jit(solution)/shard_map/ptq,ptd->pqd/dot_general | solution.py:185
  139.8 3.8 fusion.6
  143.9 0.9 fusion.26
  146.4 4.9 %copy.153 = bf16[512,8,2,256]{3,1,2,0:T(8,128)(2,1)} copy(bf16[512,8,2,256]{3,2,1,0:T(2,128)(2,1)} %bitcast.232) | data formatting | bytes 8388608
  151.2 1.0 scatter_custom_fusion.2
  152.4 3.8 fusion.10
  157.0 22.3 %all_gather.13 = f32[32,4,16,1,4]{2,4,3,1,0:T(4,128)S(1)} all-gather(f32[1,4,16,1,4]{2,4,3,1,0:T(4,128)S(1)} %get-tuple-element.113), channel_id=1, replica_groups=mesh['kv'=8,'blk'=32] {'blk'}, dimensions={0}, use_global_device_ids=true | all-gather | bytes 33792 | tf_op jit(solution)/shard_map/all_gather | solution.py:24
  179.3 24.4 %all_gather.12 = f32[32,4,16,1,4]{2,4,3,1,0:T(4,128)S(1)} all-gather(f32[1,4,16,1,4]{2,4,3,1,0:T(4,128)S(1)} %get-tuple-element.114), channel_id=1, replica_groups=mesh['kv'=8,'blk'=32] {'blk'}, dimensions={0}, use_global_device_ids=true | all-gather | bytes 33792 | tf_op jit(solution)/shard_map/all_gather | solution.py:24
  203.8 0.9 slice_bitcast_fusion.2
  204.7 4.7 %slice.137 = f32[124,16,4,128]{3,1,2,0:T(8,128)} slice(f32[128,16,4,128]{3,1,2,0:T(8,128)} %all-gather.3.cloned.1.call-done), slice={[4:128], [0:16], [0:4], [0:128]} | slice | bytes 8126464 | tf_op jit(solution)/shard_map/slice | solution.py:26
  209.4 50.2 %while.14 = (s32[]{:T(128)}, f32[4,16,1,4]{1,3,2,0:T(4,128)S(1)}, f32[4,16,1,4]{1,3,2,0:T(4,128)S(1)}, f32[4,16,1,4,128]{4,3,2,1,0:T(4,128)S(1)}, f32[31,4,16,1,...) while((s32[]{:T(128)}, f32[4,16,1,4]{1,3,2,0:T(4,128)S(1)}, ...), condition=%wide.region_11.12_spmd, body=%wide.region_10.11_spmd.sunk | while | flops 100098 | bytes 674921 | solution.py:27
  209.7 0.9 constant_dynamic-slice_fusion.2
  211.3 0.9 constant_dynamic-slice_fusion.2
  212.9 0.9 constant_dynamic-slice_fusion.2
  214.5 0.9 constant_dynamic-slice_fusion.2
  216.1 0.9 constant_dynamic-slice_fusion.2
  217.8 0.9 constant_dynamic-slice_fusion.2
  219.4 0.9 constant_dynamic-slice_fusion.2
  221.0 0.9 constant_dynamic-slice_fusion.2
  222.6 0.9 constant_dynamic-slice_fusion.2
  224.2 0.9 constant_dynamic-slice_fusion.2
  225.9 0.9 constant_dynamic-slice_fusion.2
  227.5 0.9 constant_dynamic-slice_fusion.2
  229.1 0.9 constant_dynamic-slice_fusion.2
  230.7 0.9 constant_dynamic-slice_fusion.2
  232.3 0.9 constant_dynamic-slice_fusion.2
  233.9 0.9 constant_dynamic-slice_fusion.2
  235.6 0.9 constant_dynamic-slice_fusion.2
  237.2 0.9 constant_dynamic-slice_fusion.2
  238.8 0.9 constant_dynamic-slice_fusion.2
  240.4 0.9 constant_dynamic-slice_fusion.2
  242.0 0.9 constant_dynamic-slice_fusion.2
  243.7 0.9 constant_dynamic-slice_fusion.2
  245.3 0.9 constant_dynamic-slice_fusion.2
  246.9 0.9 constant_dynamic-slice_fusion.2
  248.5 0.9 constant_dynamic-slice_fusion.2
  250.1 0.9 constant_dynamic-slice_fusion.2
  251.8 0.9 constant_dynamic-slice_fusion.2
  253.4 0.9 constant_dynamic-slice_fusion.2
  255.0 0.9 constant_dynamic-slice_fusion.2
  256.6 0.9 constant_dynamic-slice_fusion.2
  258.2 0.9 constant_dynamic-slice_fusion.2
  260.0 30.2 %psum.30 = f32[64,128]{1,0:T(8,128)S(1)} all-reduce(f32[64,128]{1,0:T(8,128)S(1)} %fusion.38), channel_id=1, replica_groups=mesh['kv'=8,'blk'=32] {'kv'}, use_global_device_ids=true, to_apply=%region_12.13 | all-reduce | flops 8192 | bytes 65536 | tf_op jit(solution)/shard_map/psum | solution.py:74
  290.2 22.5 %all_gather.15 = bf16[64,4096]{1,0:T(8,128)(2,1)S(1)} all-gather(bf16[64,128]{1,0:T(8,128)(2,1)S(1)} %fusion.56), channel_id=1, replica_groups=mesh['kv'=8,'blk'=32] {'blk'}, dimensions={1}, use_global_device_ids=true | all-gather | bytes 540672 | tf_op jit(solution)/shard_map/all_gather | solution.py:266
  313.6 2.8 fusion.28
  316.5 1.1 fusion.15
  318.0 1.0 scatter_custom_fusion.4
  319.1 1.0 scatter_custom_fusion.3
  320.3 75.3 %reduce-scatter.2.cloned.1.call-done = f32[24,128]{1,0:T(8,128)} async-done(((f32[24,4096]{1,0:T(8,128)}), f32[24,128]{1,0:T(8,128)}) %reduce-scatter.2.cloned.1.call-update) | async-done | bytes 12304 | tf_op jit(solution)/shard_map/reduce_scatter | solution.py:285
  395.7 0.9 fusion.59
  396.6 30.2 %psum.31 = f32[64,128]{1,0:T(8,128)S(1)} all-reduce(f32[64,128]{1,0:T(8,128)S(1)} %fusion.59), channel_id=1, replica_groups=mesh['kv'=8,'blk'=32] {'kv'}, use_global_device_ids=true, to_apply=%region_22.23 | all-reduce | flops 8192 | bytes 65536 | tf_op jit(solution)/shard_map/psum | solution.py:74
  (333 shorter events, 38.4 us)
Async XLA Ops:
  6.5 309.9 %copy-start = (bf16[1,256,4096]{2,1,0:T(8,128)(2,1)S(1)}, bf16[1,256,4096]{2,1,0:T(8,128)(2,1)}, u32[]{:S(2)}) copy-start(bf16[1,256,4096]{2,1,0:T(8,128)(2,1)} %param.22) | copy-start | bytes 6291460
  6.5 117.8 %all-reduce.2.cloned.1.call-start = ((), (), s32[]{:S(2)}) async-start(), calls=%async_computation.1 | async-start | bytes 393216 | tf_op jit(solution)/shard_map/psum | solution.py:124
  10.0 193.8 %all-gather.3.cloned.1.call-start = ((), (), s32[]{:S(2)}) async-start(), calls=%async_computation.3 | async-start | bytes 4325376 | tf_op jit(solution)/shard_map/all_gather | solution.py:24
  139.7 5.3 %copy-start.4 = (bf16[4096]{0:T(1024)(128)(2,1)S(1)}, bf16[4096]{0:T(1024)(128)(2,1)}, u32[]{:S(2)}) copy-start(bf16[4096]{0:T(1024)(128)(2,1)} %param.17) | copy-start | bytes 24580
  139.7 5.3 %copy-start.3 = (s32[4,16,2]{1,2,0:T(2,128)S(1)}, s32[4,16,2]{1,2,0:T(2,128)}, u32[]{:S(2)}) copy-start(s32[4,16,2]{1,2,0:T(2,128)} %param.27) | copy-start | bytes 1540
  144.8 250.9 %reduce-scatter.2.cloned.1.call-start = ((), (), s32[]{:S(2)}) async-start(), calls=%async_computation.2 | async-start | bytes 405504 | tf_op jit(solution)/shard_map/reduce_scatter | solution.py:285
  209.4 50.4 %copy-start.1 = (bf16[512,128]{1,0:T(8,128)(2,1)S(1)}, bf16[512,128]{1,0:T(8,128)(2,1)}, u32[]{:S(2)}) copy-start(bf16[512,128]{1,0:T(8,128)(2,1)} %param.19) | copy-start | bytes 393220
  209.4 80.8 %copy-start.2 = (bf16[4,16,128]{2,1,0:T(8,128)(2,1)S(1)}, bf16[4,16,128]{2,1,0:T(8,128)(2,1)}, u32[]{:S(2)}) copy-start(bf16[4,16,128]{2,1,0:T(8,128)(2,1)} %param.15) | copy-start | bytes 49156
  313.4 6.6 %copy-start.5 = (bf16[4096,8]{0,1:T(8,128)(2,1)S(1)}, bf16[4096,8]{0,1:T(8,128)(2,1)}, u32[]{:S(2)}) copy-start(bf16[4096,8]{0,1:T(8,128)(2,1)} %param.20) | copy-start | bytes 196612
Sparse Core Ops, SparseCore 0:
  10.6 113.7 all-reduce.1
  144.9 49.8 all-gather.2
  317.7 77.8 reduce-scatter.1
where the time goes:
time: 435 us; the launch traced here: 434 us
  blocking collectives  192 us (44%)
  waiting for transfers between devices  96.8 us (22%)
  local copies, waits for them, and re-layouts  80.5 us (19%)
  other arithmetic  27.1 us (6%)
  matrix products  22.6 us (5%)
  between operations  13.7 us (3%)
    reduce_scatter x1, waiting for transfers between devices, body(): lax.psum_scatter(down_part, 'blk', scatter_dimension=1, tiled=True)  75.3 us
    psum x1, blocking collectives, body(): projected_rows, square_sum = lax.psum((partial_proj, partial_sq), 'blk')  62.3 us
    psum x2, blocking collectives, head_total(): return lax.psum(partial_value, 'kv')  60.4 us
    all_gather x2, blocking collectives, joined(): pieces = jax.tree.map(lambda part: lax.all_gather(part, axis), value)  46.7 us
    dynamic_slice x31, local copies, waits for them, and re-layouts, joined(): lax.scan(lambda running, section: (join(running, section), None), head, t...  28.3 us
    all_gather x1, blocking collectives, body(): full_rows = lax.all_gather(residual, 'blk', axis=1, tiled=True)  22.5 us
    psum x1, waiting for transfers between devices, body(): projected_rows, square_sum = lax.psum((partial_proj, partial_sq), 'blk')  21.4 us
    add x31, other arithmetic, combine_parts(): vector_one * scale_one[..., None] + vector_two * scale_two[..., None]  13.1 us
  transfers between devices with their start and end apart: 3, of which 2 were waited for; matrix products, arithmetic and copies ran while one was open for 10% of the time, Pallas kernels for 0%

commit v1 on v0

--- a/solution.py
+++ b/solution.py
@@ -263,7 +263,10 @@
     row_own = (row_start + jnp.arange(rows_local, dtype=jnp.int32)) // rows_per_expert
     in_flat = expert_in.reshape(experts_local, MODEL_WIDTH, 2 * ff_local)
     gain_wide = ffn_gain.astype(jnp.float32)
-    full_rows = lax.all_gather(residual, "blk", axis=1, tiled=True)
+    w1 = lax.axis_size("blk")
+    moved = jnp.stack(w1 * [residual], 0)
+    p_next = lax.all_to_all(moved, axis_name="blk", split_axis=0, concat_axis=0)
+    full_rows = jnp.concatenate(p_next, 1)
     chosen = full_rows[row_token].astype(jnp.float32)
     pre_rows = (chosen * gain_wide).astype(jnp.bfloat16)
     sums_in = jnp.einsum(

time: 435 us -> 422 us (0.970)
  blocking collectives: 192 us -> 170 us
  starting transfers between devices: 0.27 us -> 5.25 us
    all_gather x1 -> x0, blocking collectives: 22.5 us -> none  [body(): full_rows = lax.all_gather(residual, 'blk', axis=1, tiled=True)]
    all_to_all x0 -> x1, starting transfers between devices: none -> 5.17 us  [body(): p_next = lax.all_to_all(moved, axis_name='blk', split_axis=0, concat_axis=0)]
  transfers between devices with their start and end apart: 3 -> 4, of which waited for: 2 -> 3; matrix products, arithmetic and copies ran while one was open for 10% -> 11% of each run, Pallas kernels for 0% -> 0%
where the time goes in v1:
time: 422 us; the launch traced here: 421 us
  blocking collectives  170 us (40%)
  waiting for transfers between devices  99.7 us (24%)
  local copies, waits for them, and re-layouts  81.5 us (19%)
  other arithmetic  27.1 us (6%)
  matrix products  22.6 us (5%)
  between operations  13.7 us (3%)
  starting transfers between devices  5.25 us (1%)
    reduce_scatter x1, waiting for transfers between devices, body(): lax.psum_scatter(down_part, 'blk', scatter_dimension=1, tiled=True)  74.3 us
    psum x1, blocking collectives, body(): projected_rows, square_sum = lax.psum((partial_proj, partial_sq), 'blk')  62.4 us
    psum x2, blocking collectives, head_total(): return lax.psum(partial_value, 'kv')  60.5 us
    all_gather x2, blocking collectives, joined(): pieces = jax.tree.map(lambda part: lax.all_gather(part, axis), value)  47 us
    dynamic_slice x31, local copies, waits for them, and re-layouts, joined(): lax.scan(lambda running, section: (join(running, section), None), head, t...  28.3 us
    psum x1, waiting for transfers between devices, body(): projected_rows, square_sum = lax.psum((partial_proj, partial_sq), 'blk')  21.2 us
    add x31, other arithmetic, combine_parts(): vector_one * scale_one[..., None] + vector_two * scale_two[..., None]  13.1 us
  transfers between devices with their start and end apart: 4, of which 3 were waited for; matrix products, arithmetic and copies ran while one was open for 11% of the time, Pallas kernels for 0%

profile of v1, /device:TPU:2, one launch (start us, length us, event | category | flops | bytes accessed | tf_op | source)
XLA Modules:
  0.0 420.8 jit_solution(6033154783263802793)
XLA Ops:
  8.2 1.8 fusion.31
  10.0 1.3 fusion.108
  12.1 8.0 %scatter_custom_fusion = s32[2048]{0:T(1024)S(1)} fusion(s32[2048]{0:T(1024)S(1)} %bitcast.255, s32[2048]{0:T(1024)S(1)} %add_select_fusion, s32[]{:T(128)} %constant.125.clone.1), kind=kCustom, calls=%fused_computation.169 | custom fusion | bytes 8196 | tf_op jit(solution)/shard_map/scatter | solution.py:143
  20.1 8.0 %scatter_custom_fusion.1 = s32[2048]{0:T(1024)S(1)} fusion(s32[2048]{0:T(1024)S(1)} %bitcast.256, s32[2048]{0:T(1024)S(1)} %fusion.64, s32[]{:T(128)} %constant.125.clone.1), kind=kCustom, calls=%fused_computation.167 | custom fusion | bytes 8196 | tf_op jit(solution)/shard_map/scatter | solution.py:148
  28.2 1.3 fusion.86
  29.5 1.4 compare_select_fusion.12
  39.1 62.4 %psum.29 = f32[64]{0:T(128)S(1)} all-reduce(f32[64]{0:T(128)S(1)} %reduce_sum.66), channel_id=1, replica_groups=mesh['kv'=8,'blk'=32] {'blk'}, use_global_device_ids=true, to_apply=%region_4.5 | all-reduce | flops 64 | bytes 512 | tf_op jit(solution)/shard_map/psum | solution.py:124
  103.2 21.2 %all-reduce.2.cloned.1.call-done = f32[64,768]{1,0:T(8,128)} async-done(((f32[64,768]{1,0:T(8,128)}), f32[64,768]{1,0:T(8,128)}) %all-reduce.2.cloned.1.call-update) | async-done | bytes 196624 | tf_op jit(solution)/shard_map/psum | solution.py:124
  124.4 1.0 broadcast_multiply_fusion
  125.9 2.2 gather_fusion.11
  128.1 4.7 %fusion.8 = (f32[64,128]{1,0:T(8,128)S(1)}, f32[64,128,128]{1,2,0:T(8,128)}) fusion(pred[64,128]{1,0:T(8,128)(4,1)S(1)} %broadcast_compare_fusion.1, pred[64,128]{1,0:T(8,128)(4,1)S(1)} %add_compare_fusion, bf16[64,128,128]{2,1,0:T(8,128)(2,1)} %gather_fusion.11, bf16[64,2,1,128,128]{4,3,2,1,0:T(8,128)(2,1)} %param.23), kind=kOutput, calls=%fused_computation.35 | convolution fusion | flops 272621568 | bytes 8437760 | tf_op jit(solution)/shard_map/ptd,pqd->ptq/dot_general | solution.py:177
  134.0 5.8 %convolution_multiply_fusion = f32[64,128,128]{2,1,0:T(8,128)S(1)} fusion(f32[64,128,128]{1,2,0:T(8,128)} %get-tuple-element.131, f32[64,128]{1,0:T(8,128)S(1)} %subtract_exponential_fusion.1, bf16[64,2,1,128,128]{4,3,2,1,0:T(8,128)(2,1)} %param.23, f32[64,128]{1,0:T(8,128)S(1)} %get-tuple-element.130, pred[64,128]{1,0:T(8,128)(4,1)S(1)} %broadcast_compare_fusion.1, ...), kind=kOutput, calls=%fused_computation.38 | convolution fusion | flops 275775488 | bytes 10567680 | tf_op jit(solution)/shard_map/ptq,ptd->pqd/dot_general | solution.py:185
  139.9 3.8 fusion.6
  144.0 0.9 fusion.26
  146.0 3.8 fusion.10
  150.6 22.3 %all_gather.10 = f32[32,4,16,1,4]{2,4,3,1,0:T(4,128)S(1)} all-gather(f32[1,4,16,1,4]{2,4,3,1,0:T(4,128)S(1)} %get-tuple-element.113), channel_id=1, replica_groups=mesh['kv'=8,'blk'=32] {'blk'}, dimensions={0}, use_global_device_ids=true | all-gather | bytes 33792 | tf_op jit(solution)/shard_map/all_gather | solution.py:24
  172.9 24.6 %all_gather.9 = f32[32,4,16,1,4]{2,4,3,1,0:T(4,128)S(1)} all-gather(f32[1,4,16,1,4]{2,4,3,1,0:T(4,128)S(1)} %get-tuple-element.114), channel_id=1, replica_groups=mesh['kv'=8,'blk'=32] {'blk'}, dimensions={0}, use_global_device_ids=true | all-gather | bytes 33792 | tf_op jit(solution)/shard_map/all_gather | solution.py:24
  197.6 0.9 slice_bitcast_fusion.2
  198.6 4.6 %slice.137 = f32[124,16,4,128]{3,1,2,0:T(8,128)} slice(f32[128,16,4,128]{3,1,2,0:T(8,128)} %all-gather.3.cloned.1.call-done), slice={[4:128], [0:16], [0:4], [0:128]} | slice | bytes 8126464 | tf_op jit(solution)/shard_map/slice | solution.py:26
  203.2 50.2 %while.14 = (s32[]{:T(128)}, f32[4,16,1,4]{1,3,2,0:T(4,128)S(1)}, f32[4,16,1,4]{1,3,2,0:T(4,128)S(1)}, f32[4,16,1,4,128]{4,3,2,1,0:T(4,128)S(1)}, f32[31,4,16,1,...) while((s32[]{:T(128)}, f32[4,16,1,4]{1,3,2,0:T(4,128)S(1)}, ...), condition=%wide.region_11.12_spmd, body=%wide.region_10.11_spmd.sunk | while | flops 100098 | bytes 674921 | solution.py:27
  203.5 0.9 constant_dynamic-slice_fusion.2
  205.1 0.9 constant_dynamic-slice_fusion.2
  206.7 0.9 constant_dynamic-slice_fusion.2
  208.4 0.9 constant_dynamic-slice_fusion.2
  210.0 0.9 constant_dynamic-slice_fusion.2
  211.6 0.9 constant_dynamic-slice_fusion.2
  213.2 0.9 constant_dynamic-slice_fusion.2
  214.8 0.9 constant_dynamic-slice_fusion.2
  216.4 0.9 constant_dynamic-slice_fusion.2
  218.1 0.9 constant_dynamic-slice_fusion.2
  219.7 0.9 constant_dynamic-slice_fusion.2
  221.3 0.9 constant_dynamic-slice_fusion.2
  222.9 0.9 constant_dynamic-slice_fusion.2
  224.5 0.9 constant_dynamic-slice_fusion.2
  226.2 0.9 constant_dynamic-slice_fusion.2
  227.8 0.9 constant_dynamic-slice_fusion.2
  229.4 0.9 constant_dynamic-slice_fusion.2
  231.0 0.9 constant_dynamic-slice_fusion.2
  232.6 0.9 constant_dynamic-slice_fusion.2
  234.3 0.9 constant_dynamic-slice_fusion.2
  235.9 0.9 constant_dynamic-slice_fusion.2
  237.5 0.9 constant_dynamic-slice_fusion.2
  239.1 0.9 constant_dynamic-slice_fusion.2
  240.7 0.9 constant_dynamic-slice_fusion.2
  242.4 0.9 constant_dynamic-slice_fusion.2
  244.0 0.9 constant_dynamic-slice_fusion.2
  245.6 0.9 constant_dynamic-slice_fusion.2
  247.2 0.9 constant_dynamic-slice_fusion.2
  248.8 0.9 constant_dynamic-slice_fusion.2
  250.4 0.9 constant_dynamic-slice_fusion.2
  252.1 0.9 constant_dynamic-slice_fusion.2
  253.8 30.2 %psum.30 = f32[64,128]{1,0:T(8,128)S(1)} all-reduce(f32[64,128]{1,0:T(8,128)S(1)} %fusion.38), channel_id=1, replica_groups=mesh['kv'=8,'blk'=32] {'kv'}, use_global_device_ids=true, to_apply=%region_12.13 | all-reduce | flops 8192 | bytes 65536 | tf_op jit(solution)/shard_map/psum | solution.py:74
  284.1 0.9 stack.119
  285.0 5.2 %all-to-all-start = ((bf16[32,64,128]{2,1,0:T(8,128)(2,1)}), bf16[32,64,128]{2,1,0:T(8,128)(2,1)S(1)}, u32[]{:S(2)}, u32[]{:S(2)}) async-start(bf16[32,64,128]{2,1,0:T(8,128)(2,1)} %stack.119), calls=%async_computation | async-start | bytes 1048576 | tf_op jit(solution)/shard_map/all_to_all | solution.py:268
  290.5 4.9 %copy.156 = bf16[512,8,2,256]{3,1,2,0:T(8,128)(2,1)} copy(bf16[512,8,2,256]{3,2,1,0:T(2,128)(2,1)} %bitcast.238) | data formatting | bytes 8388608
  295.4 1.0 scatter_custom_fusion.2
  296.4 4.1 all-to-all-done
  301.4 2.8 fusion.28
  304.3 1.1 fusion.15
  305.8 1.0 scatter_custom_fusion.4
  306.9 1.0 scatter_custom_fusion.3
  308.2 74.3 %reduce-scatter.2.cloned.1.call-done = f32[24,128]{1,0:T(8,128)} async-done(((f32[24,4096]{1,0:T(8,128)}), f32[24,128]{1,0:T(8,128)}) %reduce-scatter.2.cloned.1.call-update) | async-done | bytes 12304 | tf_op jit(solution)/shard_map/reduce_scatter | solution.py:288
  382.5 0.9 fusion.59
  383.4 30.2 %psum.31 = f32[64,128]{1,0:T(8,128)S(1)} all-reduce(f32[64,128]{1,0:T(8,128)S(1)} %fusion.59), channel_id=1, replica_groups=mesh['kv'=8,'blk'=32] {'kv'}, use_global_device_ids=true, to_apply=%region_22.23 | all-reduce | flops 8192 | bytes 65536 | tf_op jit(solution)/shard_map/psum | solution.py:74
  (336 shorter events, 39.9 us)
Async XLA Ops:
  6.5 297.7 %copy-start = (bf16[1,256,4096]{2,1,0:T(8,128)(2,1)S(1)}, bf16[1,256,4096]{2,1,0:T(8,128)(2,1)}, u32[]{:S(2)}) copy-start(bf16[1,256,4096]{2,1,0:T(8,128)(2,1)} %param.22) | copy-start | bytes 6291460
  6.5 117.9 %all-reduce.2.cloned.1.call-start = ((), (), s32[]{:S(2)}) async-start(), calls=%async_computation.2 | async-start | bytes 393216 | tf_op jit(solution)/shard_map/psum | solution.py:124
  10.0 187.7 %all-gather.3.cloned.1.call-start = ((), (), s32[]{:S(2)}) async-start(), calls=%async_computation.4 | async-start | bytes 4325376 | tf_op jit(solution)/shard_map/all_gather | solution.py:24
  139.8 5.1 %copy-start.4 = (bf16[4096]{0:T(1024)(128)(2,1)S(1)}, bf16[4096]{0:T(1024)(128)(2,1)}, u32[]{:S(2)}) copy-start(bf16[4096]{0:T(1024)(128)(2,1)} %param.17) | copy-start | bytes 24580
  139.8 5.1 %copy-start.3 = (s32[4,16,2]{1,2,0:T(2,128)S(1)}, s32[4,16,2]{1,2,0:T(2,128)}, u32[]{:S(2)}) copy-start(s32[4,16,2]{1,2,0:T(2,128)} %param.27) | copy-start | bytes 1540
  203.2 50.4 %copy-start.1 = (bf16[512,128]{1,0:T(8,128)(2,1)S(1)}, bf16[512,128]{1,0:T(8,128)(2,1)}, u32[]{:S(2)}) copy-start(bf16[512,128]{1,0:T(8,128)(2,1)} %param.19) | copy-start | bytes 393220
  203.2 80.8 %copy-start.2 = (bf16[4,16,128]{2,1,0:T(8,128)(2,1)S(1)}, bf16[4,16,128]{2,1,0:T(8,128)(2,1)}, u32[]{:S(2)}) copy-start(bf16[4,16,128]{2,1,0:T(8,128)(2,1)} %param.15) | copy-start | bytes 49156
  285.0 15.6 %all-to-all-start = ((bf16[32,64,128]{2,1,0:T(8,128)(2,1)}), bf16[32,64,128]{2,1,0:T(8,128)(2,1)S(1)}, u32[]{:S(2)}, u32[]{:S(2)}) async-start(bf16[32,64,128]{2,1,0:T(8,128)(2,1)} %stack.119), calls=%async_computation | async-start | bytes 1048576 | tf_op jit(solution)/shard_map/all_to_all | solution.py:268
  290.1 92.4 %reduce-scatter.2.cloned.1.call-start = ((), (), s32[]{:S(2)}) async-start(), calls=%async_computation.3 | async-start | bytes 405504 | tf_op jit(solution)/shard_map/reduce_scatter | solution.py:288
  301.3 6.6 %copy-start.5 = (bf16[4096,8]{0,1:T(8,128)(2,1)S(1)}, bf16[4096,8]{0,1:T(8,128)(2,1)}, u32[]{:S(2)}) copy-start(bf16[4096,8]{0,1:T(8,128)(2,1)} %param.20) | copy-start | bytes 196612
Sparse Core Ops, SparseCore 0:
  10.6 113.7 all-reduce.1
  145.0 49.9 all-gather.2
  305.6 76.8 reduce-scatter.1
